TPU v7x, 256 devices: a whole 4x4x8 slice. The times are simulated.
256 devices in a mesh: dp: 16 (over x, y), expert: 16 (over z, core).
Axes of the slice: x: 4, y: 4, z: 8, core: 2. Of those that a mesh axis runs over, the one named last changes fastest.
Arguments:
- hidden: bfloat16 [32768, 8, 768], P(('dp', 'expert')), may hold values from -6 to 6
- upstream: bfloat16 [32768, 4096], P(('dp', 'expert')), may hold values from -0.125 to 0.125
- probs: bfloat16 [32768, 8], P(('dp', 'expert')), may hold values from 0.019897461 to 0.5
- expert_ids: int32 [32768, 8], P(('dp', 'expert')), may hold values from 0 to 15, all different within a row; in each aligned block of 128 rows (0 to 127, 128 to 255, ...) at most 72 rows name the same one
- w_down: bfloat16 [16, 4096, 768], P('expert', 'dp'), may hold values from -0.21875 to 0.21875
Outputs:
- grad_down: float32 [16, 4096, 768], P('expert', 'dp')
- gate_grad: float32 [32768, 8], P(('dp', 'expert'))
Inputs may be any that keep to these rules, and one draw needn't show every extreme that they name: `expert_ids`: each row names 8 different experts; among the rows of one device no expert is named by more than 72 rows, a bound that some block reaches.
All inputs are finite; a program needn't handle non-finite values.
Results may differ from a plain program's by a relative error of at most 0.013.
Values may be sent and summed in bfloat16 or wider, within the bound.
No kernel may reach another device: no remote copies, remote signals or barrier semaphores. Data moves between devices by JAX's collectives and lax.ppermute only.
A program may use at most 128 MiB of HBM per device.

v0:
```python
import jax
import jax.numpy as jnp
from jax import lax
from jax.sharding import Mesh, PartitionSpec as P


def body(hidden, upstream, probs, expert_ids, w_down):
    tok_rows, top_k = expert_ids.shape
    hid_width = hidden.shape[2]
    model_width = upstream.shape[1]
    n_z = lax.axis_size("z")
    n_core = lax.axis_size("core")
    n_dp = lax.axis_size("x") * lax.axis_size("y")
    groups = n_z * n_core
    slots_per = max(tok_rows * 9 // 16, tok_rows * top_k // groups)
    total_rows = groups * slots_per
    ez = ("z", "core")
    chosen = (expert_ids[:, :, None] == jnp.arange(groups, dtype=jnp.int32)[None, None, :]).astype(
        jnp.int32
    )
    member = jnp.sum(chosen, axis=1)
    slot_place = jnp.cumsum(member, axis=0) - 1
    which_k = jnp.sum(chosen * jnp.arange(top_k, dtype=jnp.int32)[None, :, None], axis=1)
    target = (
        (member == 1)[:, :, None]
        & (slot_place[:, :, None] == jnp.arange(slots_per, dtype=jnp.int32)[None, None, :])
    ).astype(jnp.int32)
    filled = jnp.sum(target, axis=0) == 1
    source_tok = jnp.sum(target * jnp.arange(tok_rows, dtype=jnp.int32)[:, None, None], axis=0)
    source_k = jnp.sum(target * which_k[:, :, None], axis=0)
    flat_index = (source_tok * top_k + source_k).reshape(-1)
    picked_h = hidden.reshape(tok_rows * top_k, hid_width)[flat_index].reshape(
        groups, slots_per, hid_width
    )
    send_h = jnp.where(filled[:, :, None], picked_h, jnp.zeros_like(picked_h))
    routed = member == 1
    p_tok = jnp.sum(
        jnp.where(chosen == 1, probs.astype(jnp.float32)[:, :, None], jnp.float32(0.0)), axis=1
    )
    inv = jnp.where(routed, slot_place, -1).astype(jnp.float32)
    send_meta = jnp.stack([p_tok.T, inv.T], axis=1)
    dy_z = lax.all_gather(upstream, "z", axis=0, tiled=True)
    recv_h = lax.all_to_all(send_h, ez, split_axis=0, concat_axis=0, tiled=True)
    recv_meta = lax.all_to_all(send_meta, ez, split_axis=0, concat_axis=0, tiled=True)

    def ring_gather(x, axis):
        n = lax.axis_size(axis)
        got = [x] + [
            lax.ppermute(x, axis, perm=[(i, (i - d) % n) for i in range(n)]) for d in range(1, n)
        ]
        return jnp.roll(jnp.stack(got), lax.axis_index(axis), axis=0)

    w_full = ring_gather(ring_gather(w_down[0], "y"), "x")
    dy_z, w_full, recv_h, recv_meta = lax.optimization_barrier((dy_z, w_full, recv_h, recv_meta))
    w_full = w_full.reshape(-1, hid_width)
    dy_pair = lax.ppermute(dy_z, "core", perm=[(c, (c + 1) % n_core) for c in range(n_core)])
    my_core = lax.axis_index("core")
    other_core = (my_core + 1) % n_core

    def inputs(c):
        meta = lax.dynamic_index_in_dim(
            recv_meta.reshape(n_z, n_core, 2, tok_rows), c, axis=1, keepdims=False
        )
        p_c = meta[:, 0, :].reshape(-1)
        slot = meta[:, 1, :].astype(jnp.int32)
        h_src = lax.dynamic_index_in_dim(
            recv_h.reshape(n_z, n_core, slots_per, hid_width), c, axis=1, keepdims=False
        )
        pick = (slot[:, :, None] == jnp.arange(slots_per, dtype=jnp.int32)[None, None, :]).astype(
            h_src.dtype
        )
        h_c = lax.dot_general(
            pick, h_src, (((2,), (1,)), ((0,), (0,))), preferred_element_type=jnp.float32
        ).astype(h_src.dtype)
        return (p_c, h_c.reshape(n_z * tok_rows, hid_width))

    p_own, h_own = inputs(my_core)
    p_pair, h_pair = inputs(other_core)

    def part(dy_c, p_c, h_c):
        scaled = (p_c[:, None] * dy_c.astype(jnp.float32)).astype(jnp.bfloat16)
        return lax.dot_general(
            scaled, h_c, (((0,), (0,)), ((), ())), preferred_element_type=jnp.float32
        )

    def score(dy_c, h_c):
        g = lax.dot_general(
            dy_c, w_full, (((1,), (0,)), ((), ())), preferred_element_type=jnp.float32
        )
        return jnp.sum(g * h_c.astype(jnp.float32), axis=1).reshape(n_z, tok_rows)

    partial = (part(dy_z, p_own, h_own) + part(dy_pair, p_pair, h_pair)).astype(jnp.bfloat16)
    grad_block = lax.psum_scatter(partial, ("x", "y"), scatter_dimension=0, tiled=True).astype(
        jnp.float32
    )
    score_own = score(dy_z, h_own)
    score_pair = score(dy_pair, h_pair)
    first = jnp.where(my_core == 0, score_own, score_pair)
    second = jnp.where(my_core == 0, score_pair, score_own)
    by_source = jnp.stack([first, second], axis=1).reshape(groups, tok_rows)
    returned = lax.all_to_all(by_source, ez, split_axis=0, concat_axis=0, tiled=True)
    gate_grad = jnp.sum(
        jnp.where(
            expert_ids[:, :, None] == jnp.arange(groups, dtype=jnp.int32)[None, None, :],
            returned.T[:, None, :],
            jnp.float32(0.0),
        ),
        axis=2,
    )
    return (grad_block[None], gate_grad)


def solution(mesh):
    n_dp, n_expert = mesh.devices.shape
    side = 4 if n_dp % 4 == 0 else 1
    sub = Mesh(mesh.devices.reshape(n_dp // side, side, n_expert // 2, 2), ("x", "y", "z", "core"))
    tok = ("x", "y", "z", "core")
    in_specs = (
        P(tok, None, None),
        P(tok, None),
        P(tok, None),
        P(tok, None),
        P(("z", "core"), ("x", "y"), None),
    )
    out_specs = (P(("z", "core"), ("x", "y"), None), P(tok, None))
    return jax.shard_map(body, mesh=sub, in_specs=in_specs, out_specs=out_specs, check_vma=False)
```

profile of v0, /device:TPU:1, one launch (start us, length us, event | category | flops | bytes accessed | tf_op | source)
XLA Modules:
  0.0 267.1 jit_solution(8966174074436116329)
XLA Ops:
  7.9 3.6 %collective-permute-start = (bf16[256,768]{1,0:T(8,128)(2,1)}, bf16[256,768]{1,0:T(8,128)(2,1)S(1)}, u32[]{:S(2)}, u32[]{:S(2)}) collective-permute-start(bf16[256,768]{1,0:T(8,128)(2,1)} %bitcast.81), channel_id=1, source_target_pairs={{0,48},{16,0},{32,16},{48,32},{1,49},{17,1},{33,17},{49,33},{2,50}... | collective-permute-start | bytes 1179656 | tf_op jit(solution)/shard_map/ppermute | solution.py:49
  12.6 0.7 convert_reduce_fusion.1
  14.1 0.7 select_reduce_fusion.3
  15.8 10.0 %all-to-all-start.1 = ((f32[16,2,128]{2,1,0:T(2,128)}), f32[16,2,128]{2,1,0:T(2,128)S(1)}, u32[]{:S(2)}, u32[]{:S(2)}) async-start(f32[16,2,128]{2,1,0:T(2,128)} %copy.33), calls=%async_computation.1 | async-start | bytes 32768 | tf_op jit(solution)/shard_map/all_to_all | solution.py:44
  25.9 0.9 convert_reduce_fusion
  27.0 1.0 constant_dynamic-update-slice_fusion.1
  28.1 4.8 %collective-permute-done.2 = bf16[256,768]{1,0:T(8,128)(2,1)S(1)} collective-permute-done((bf16[256,768]{1,0:T(8,128)(2,1)}, bf16[256,768]{1,0:T(8,128)(2,1)S(1)}, u32[]{:S(2)}, u32[]{:S(2)}) %collective-permute-start.2) | collective-permute-done | bytes 393248 | tf_op jit(solution)/shard_map/ppermute | solution.py:49
  33.0 1.9 bitcast_dynamic-update-slice_fusion.6
  34.9 2.5 collective-permute-start.3
  38.1 4.6 %gather_fusion = bf16[1152,768]{1,0:T(8,128)(2,1)S(1)} fusion(bf16[1024,768]{1,0:T(8,128)(2,1)S(1)} %bitcast.71, s32[2048]{0:T(1024)S(1)} %pad_clamp_fusion), kind=kCustom, calls=%fused_computation | custom fusion | bytes 3543552 | tf_op jit(solution)/shard_map/gather | solution.py:32
  43.3 1.4 broadcast_select_fusion
  44.7 9.7 %all-to-all-start = ((bf16[16,72,768]{2,1,0:T(8,128)(2,1)}), bf16[16,72,768]{2,1,0:T(8,128)(2,1)S(1)}, u32[]{:S(2)}, u32[]{:S(2)}) async-start(bf16[16,72,768]{2,1,0:T(8,128)(2,1)} %broadcast_select_fusion), calls=%async_computation | async-start | bytes 3538944 | tf_op jit(solution)/shard_map/all_to_all | solution.py:43
  54.5 50.2 %collective-permute-done.3 = bf16[4,256,768]{2,1,0:T(8,128)(2,1)} collective-permute-done((bf16[4,256,768]{2,1,0:T(8,128)(2,1)}, bf16[4,256,768]{2,1,0:T(8,128)(2,1)}, u32[]{:S(2)}, u32[]{:S(2)}) %collective-permute-start.3) | collective-permute-done | bytes 1572896 | tf_op jit(solution)/shard_map/ppermute | solution.py:49
  104.7 2.7 bitcast_dynamic-update-slice_fusion.4
  107.3 2.6 bitcast_dynamic-update-slice_fusion.2
  110.0 1.3 bitcast_dynamic-update-slice_fusion
  111.3 2.7 %bitcast_dynamic-update-slice_fusion.7 = bf16[8,4,256,768]{3,2,1,0:T(8,128)(2,1)} fusion(bf16[8,4,256,768]{3,2,1,0:T(8,128)(2,1)} %bitcast_dynamic-update-slice_fusion, bf16[4,256,768]{2,1,0:T(8,128)(2,1)} %get-tuple-element.18), kind=kLoop, calls=%fused_computation.20 | loop fusion | bytes 3145728
  113.9 2.7 %bitcast_dynamic-update-slice_fusion.5 = bf16[8,4,256,768]{3,2,1,0:T(8,128)(2,1)} fusion(bf16[8,4,256,768]{3,2,1,0:T(8,128)(2,1)} %bitcast_dynamic-update-slice_fusion.7, bf16[4,256,768]{2,1,0:T(8,128)(2,1)} %collective-permute-done.3), kind=kLoop, calls=%fused_computation.18 | loop fusion | bytes 3145728
  116.7 2.7 %bitcast_dynamic-update-slice_fusion.3 = bf16[8,4,256,768]{3,2,1,0:T(8,128)(2,1)} fusion(bf16[8,4,256,768]{3,2,1,0:T(8,128)(2,1)} %bitcast_dynamic-update-slice_fusion.5, bf16[4,256,768]{2,1,0:T(8,128)(2,1)} %collective-permute-done.4), kind=kLoop, calls=%fused_computation.16 | loop fusion | bytes 3145728
  119.4 1.2 bitcast_dynamic-update-slice_fusion.1
  120.6 6.1 %constant_dynamic-slice_fusion.2 = bf16[4,4,256,768]{3,2,1,0:T(8,128)(2,1)} fusion(bf16[8,4,256,768]{3,2,1,0:T(8,128)(2,1)} %bitcast_dynamic-update-slice_fusion.1, s32[]{:T(128)S(6)} %select_n.102), kind=kLoop, calls=%fused_computation.71 | loop fusion | bytes 12582916 | tf_op jit(solution)/shard_map/jit(_roll_dynamic)/dynamic_slice | solution.py:51
  126.7 19.4 %all-gather.2.cloned.1.call-done = bf16[1024,4096]{1,0:T(8,128)(2,1)} async-done(((bf16[128,4096]{1,0:T(8,128)(2,1)}), bf16[1024,4096]{1,0:T(8,128)(2,1)}) %all-gather.2.cloned.1.call-update) | async-done | bytes 8388624 | tf_op jit(solution)/shard_map/all_gather | solution.py:42
  148.1 10.8 %fusion = f32[4096,768]{1,0:T(8,128)S(1)} fusion(bf16[1024,768]{1,0:T(8,128)(2,1)S(1)} %bitcast.79, bf16[1024,4096]{1,0:T(8,128)(2,1)} %all-gather.2.cloned.1.call-done, f32[1024]{0:T(1024)S(1)} %get-tuple-element.26), kind=kOutput, calls=%fused_computation.4 | convolution fusion | flops 6455033856 | bytes 22548480 | tf_op jit(solution)/shard_map/dot_general | solution.py:82
  158.8 1.0 collective-permute-done.6
  159.9 14.7 %add_convert_fusion = bf16[4096,768]{1,0:T(8,128)(2,1)} fusion(f32[4096,768]{1,0:T(8,128)S(1)} %fusion, bf16[1024,768]{1,0:T(8,128)(2,1)S(1)} %bitcast.77, bf16[1024,4096]{1,0:T(8,128)(2,1)} %collective-permute-done.6, f32[1024]{0:T(1024)S(1)} %get-tuple-element.24), kind=kOutput, calls=%fused_computation.3 | convolution fusion | flops 6461325312 | bytes 28839936 | tf_op jit(solution)/shard_map/dot_general | solution.py:82
  174.6 1.6 copy.36
  176.2 0.7 copy.35
  177.0 11.1 %multiply_reduce_fusion.1 = f32[1024]{0:T(1024)S(1)} fusion(bf16[1024,768]{0,1:T(8,128)(2,1)S(1)} %copy.35, bf16[1024,4096]{1,0:T(8,128)(2,1)} %all-gather.2.cloned.1.call-done, bf16[4096,768]{1,0:T(8,128)(2,1)} %bitcast.75), kind=kOutput, calls=%fused_computation.9 | convolution fusion | flops 6444809216 | bytes 16257024 | tf_op jit(solution)/shard_map/dot_general | solution.py:87
  188.2 11.5 %multiply_reduce_fusion = f32[1024]{0:T(1024)S(1)} fusion(bf16[1024,768]{0,1:T(8,128)(2,1)S(1)} %copy-done.4, bf16[1024,4096]{1,0:T(8,128)(2,1)} %collective-permute-done.6, bf16[4096,768]{1,0:T(8,128)(2,1)} %bitcast.76), kind=kOutput, calls=%fused_computation.8 | convolution fusion | flops 6444809216 | bytes 16257024 | tf_op jit(solution)/shard_map/dot_general | solution.py:87
  199.7 11.4 %all_to_all.22 = f32[16,1,128]{2,1,0:T(1,128)S(1)} all-to-all(f32[16,1,128]{2,1,0:T(1,128)S(1)} %bitcast.86), channel_id=1, replica_groups=mesh['x'=4,'y'=4,'z'=8,'core'=2] {'z','core'}, dimensions={0} | all-to-all | bytes 16384 | tf_op jit(solution)/shard_map/all_to_all | solution.py:101
  211.7 46.6 %reduce-scatter.2.cloned.1.call-done = bf16[256,768]{1,0:T(8,128)(2,1)} async-done(((bf16[4096,768]{1,0:T(8,128)(2,1)}), bf16[256,768]{1,0:T(8,128)(2,1)}) %reduce-scatter.2.cloned.1.call-update) | async-done | bytes 393232 | tf_op jit(solution)/shard_map/reduce_scatter | solution.py:93
  258.3 1.9 bitcast_convert_fusion
  (60 shorter events, 8.0 us)
Async XLA Ops:
  7.2 30.9 %copy-start = (bf16[128,8,768]{2,1,0:T(8,128)(2,1)S(1)}, bf16[128,8,768]{2,1,0:T(8,128)(2,1)}, u32[]{:S(2)}) copy-start(bf16[128,8,768]{2,1,0:T(8,128)(2,1)} %param.5) | copy-start | bytes 4718596
  7.2 25.7 %copy-start.5 = (bf16[1,256,768]{2,1,0:T(8,128)(2,1)S(1)}, bf16[1,256,768]{2,1,0:T(8,128)(2,1)}, u32[]{:S(2)}) copy-start(bf16[1,256,768]{2,1,0:T(8,128)(2,1)} %param.9) | copy-start | bytes 1179652
  7.2 138.9 %all-gather.2.cloned.1.call-start = ((), (), s32[]{:S(2)}) async-start(), calls=%async_computation.4 | async-start | bytes 9437184 | tf_op jit(solution)/shard_map/all_gather | solution.py:42
  7.9 20.1 %collective-permute-start = (bf16[256,768]{1,0:T(8,128)(2,1)}, bf16[256,768]{1,0:T(8,128)(2,1)S(1)}, u32[]{:S(2)}, u32[]{:S(2)}) collective-permute-start(bf16[256,768]{1,0:T(8,128)(2,1)} %bitcast.81), channel_id=1, source_target_pairs={{0,48},{16,0},{32,16},{48,32},{1,49},{17,1},{33,17},{49,33},{2,50}... | collective-permute-start | bytes 1179656 | tf_op jit(solution)/shard_map/ppermute | solution.py:49
  11.6 16.5 %collective-permute-start.1 = (bf16[256,768]{1,0:T(8,128)(2,1)}, bf16[256,768]{1,0:T(8,128)(2,1)S(1)}, u32[]{:S(2)}, u32[]{:S(2)}) collective-permute-start(bf16[256,768]{1,0:T(8,128)(2,1)} %bitcast.82), channel_id=1, source_target_pairs={{0,32},{16,48},{32,0},{48,16},{1,33},{17,49},{33,1},{49,17},{2,34}... | collective-permute-start | bytes 1179656 | tf_op jit(solution)/shard_map/ppermute | solution.py:49
  11.9 20.9 %collective-permute-start.2 = (bf16[256,768]{1,0:T(8,128)(2,1)}, bf16[256,768]{1,0:T(8,128)(2,1)S(1)}, u32[]{:S(2)}, u32[]{:S(2)}) collective-permute-start(bf16[256,768]{1,0:T(8,128)(2,1)} %bitcast.83), channel_id=1, source_target_pairs={{0,16},{16,32},{32,48},{48,0},{1,17},{17,33},{33,49},{49,1},{2,18}... | collective-permute-start | bytes 1179656 | tf_op jit(solution)/shard_map/ppermute | solution.py:49
  15.8 28.9 %all-to-all-start.1 = ((f32[16,2,128]{2,1,0:T(2,128)}), f32[16,2,128]{2,1,0:T(2,128)S(1)}, u32[]{:S(2)}, u32[]{:S(2)}) async-start(f32[16,2,128]{2,1,0:T(2,128)} %copy.33), calls=%async_computation.1 | async-start | bytes 32768 | tf_op jit(solution)/shard_map/all_to_all | solution.py:44
  34.9 69.7 %collective-permute-start.3 = (bf16[4,256,768]{2,1,0:T(8,128)(2,1)}, bf16[4,256,768]{2,1,0:T(8,128)(2,1)}, u32[]{:S(2)}, u32[]{:S(2)}) collective-permute-start(bf16[4,256,768]{2,1,0:T(8,128)(2,1)} %get-tuple-element.18), channel_id=1, source_target_pairs={{0,192},{64,0},{128,64},{192,128},{1,193},{65,1},{129,65},{193,129... | collective-permute-start | bytes 4718600 | tf_op jit(solution)/shard_map/ppermute | solution.py:49
  37.4 69.9 %collective-permute-start.4 = (bf16[4,256,768]{2,1,0:T(8,128)(2,1)}, bf16[4,256,768]{2,1,0:T(8,128)(2,1)}, u32[]{:S(2)}, u32[]{:S(2)}) collective-permute-start(bf16[4,256,768]{2,1,0:T(8,128)(2,1)} %get-tuple-element.18), channel_id=1, source_target_pairs={{0,128},{64,192},{128,0},{192,64},{1,129},{65,193},{129,1},{193,65... | collective-permute-start | bytes 4718600 | tf_op jit(solution)/shard_map/ppermute | solution.py:49
  42.6 67.4 %collective-permute-start.5 = (bf16[4,256,768]{2,1,0:T(8,128)(2,1)}, bf16[4,256,768]{2,1,0:T(8,128)(2,1)S(1)}, u32[]{:S(2)}, u32[]{:S(2)}) collective-permute-start(bf16[4,256,768]{2,1,0:T(8,128)(2,1)} %get-tuple-element.18), channel_id=1, source_target_pairs={{0,64},{64,128},{128,192},{192,0},{1,65},{65,129},{129,193},{193,1... | collective-permute-start | bytes 4718600 | tf_op jit(solution)/shard_map/ppermute | solution.py:49
  44.7 81.9 %all-to-all-start = ((bf16[16,72,768]{2,1,0:T(8,128)(2,1)}), bf16[16,72,768]{2,1,0:T(8,128)(2,1)S(1)}, u32[]{:S(2)}, u32[]{:S(2)}) async-start(bf16[16,72,768]{2,1,0:T(8,128)(2,1)} %broadcast_select_fusion), calls=%async_computation | async-start | bytes 3538944 | tf_op jit(solution)/shard_map/all_to_all | solution.py:43
  54.5 203.9 %reduce-scatter.2.cloned.1.call-start = ((), (), s32[]{:S(2)}) async-start(), calls=%async_computation.5 | async-start | bytes 6684672 | tf_op jit(solution)/shard_map/reduce_scatter | solution.py:93
  146.1 13.8 %collective-permute-start.6 = (bf16[1024,4096]{1,0:T(8,128)(2,1)}, bf16[1024,4096]{1,0:T(8,128)(2,1)}, u32[]{:S(2)}, u32[]{:S(2)}) collective-permute-start(bf16[1024,4096]{1,0:T(8,128)(2,1)} %all-gather.2.cloned.1.call-done), channel_id=1, source_target_pairs={{0,1},{1,0},{2,3},{3,2},{4,5},{5,4},{6,7},{7,6},{8,9},{9,8},{10,11... | collective-permute-start | bytes 25165832 | tf_op jit(solution)/shard_map/ppermute | solution.py:56
  148.0 10.8 %copy-start.2 = (bf16[8,128,768]{2,1,0:T(8,128)(2,1)}, bf16[8,128,768]{2,1,0:T(8,128)(2,1)S(1)}, u32[]{:S(2)}) copy-start(bf16[8,128,768]{2,1,0:T(8,128)(2,1)S(1)} %convolution_convert_fusion.1) | copy-start | bytes 4718596
  174.6 1.7 copy-start.3
  177.0 11.1 %copy-start.4 = (bf16[1024,768]{0,1:T(8,128)(2,1)S(1)}, bf16[1024,768]{0,1:T(8,128)(2,1)}, u32[]{:S(2)}) copy-start(bf16[1024,768]{0,1:T(8,128)(2,1)} %copy.36) | copy-start | bytes 4718596
  188.1 23.0 %copy-start.6 = (s32[128,8]{0,1:T(8,128)S(1)}, s32[128,8]{0,1:T(8,128)}, u32[]{:S(2)}) copy-start(s32[128,8]{0,1:T(8,128)} %param.8) | copy-start | bytes 12292
  188.1 72.1 %copy-start.1 = (bf16[128,8,768]{2,1,0:T(8,128)(2,1)S(1)}, bf16[128,8,768]{2,1,0:T(8,128)(2,1)}, u32[]{:S(2)}) copy-start(bf16[128,8,768]{2,1,0:T(8,128)(2,1)} %param.5) | copy-start | bytes 4718596
Sparse Core Ops, SparseCore 0:
  9.8 136.2 all-gather.1
  174.7 83.5 reduce-scatter.1
where the time goes:
time: 268 us; the launch traced here: 267 us
  waiting for transfers between devices  123 us (46%)
  matrix products  49.3 us (18%)
  local copies, waits for them, and re-layouts  33.2 us (12%)
  starting transfers between devices  28.9 us (11%)
  between operations  14.4 us (5%)
  blocking collectives  11.4 us (4%)
  other arithmetic  7.23 us (3%)
    ppermute x6, waiting for transfers between devices, ring_gather(): lax.ppermute(x, axis, perm=[(i, (i - d) % n) for i in range(n)])  54.9 us
    reduce_scatter x1, waiting for transfers between devices, body(): lax.psum_scatter(partial, ('x', 'y'), scatter_dimension=0, tiled=True)  46.6 us
    dot_general x2, matrix products, part(): lax.dot_general(scaled, h_c, (((0,), (0,)), ((), ())), preferred_element_...  25.4 us
    dot_general x2, matrix products, score(): lax.dot_general(dy_c, w_full, (((1,), (0,)), ((), ())), preferred_element...  22.6 us
    all_gather x1, waiting for transfers between devices, body(): dy_z = lax.all_gather(upstream, 'z', axis=0, tiled=True)  19.4 us
    unnamed x28, local copies, waits for them, and re-layouts  17.8 us
    all_to_all x1, blocking collectives, body(): lax.all_to_all(by_source, ez, split_axis=0, concat_axis=0, tiled=True)  11.4 us
    all_to_all x1, starting transfers between devices, body(): lax.all_to_all(send_meta, ez, split_axis=0, concat_axis=0, tiled=True)  9.99 us
  transfers between devices with their start and end apart: 11, of which 5 were waited for; matrix products, arithmetic and copies ran while one was open for 27% of the time, Pallas kernels for 0%

commit v1 on v0

--- a/solution.py
+++ b/solution.py
@@ -39,7 +39,9 @@
     )
     inv = jnp.where(routed, slot_place, -1).astype(jnp.float32)
     send_meta = jnp.stack([p_tok.T, inv.T], axis=1)
-    dy_z = lax.all_gather(upstream, "z", axis=0, tiled=True)
+    dy_z = jnp.concatenate(
+        lax.all_to_all(jnp.stack([upstream] * lax.axis_size("z")), "z", 0, 0), axis=0
+    )
     recv_h = lax.all_to_all(send_h, ez, split_axis=0, concat_axis=0, tiled=True)
     recv_meta = lax.all_to_all(send_meta, ez, split_axis=0, concat_axis=0, tiled=True)
 

time: 268 us -> 395 us (1.47)
  waiting for transfers between devices: 123 us -> 202 us
  blocking collectives: 11.4 us -> 61 us
  starting transfers between devices: 28.9 us -> 23.1 us
  local copies, waits for them, and re-layouts: 33.2 us -> 37.4 us
    all_to_all x1, waiting for transfers between devices: 0.01 us -> 69.4 us  [body(): lax.all_to_all(jnp.stack([upstream] * lax.axis_size('z')), 'z', 0, 0)]
    all_to_all x0 -> x1, blocking collectives: none -> 51.2 us  [body(): recv_h = lax.all_to_all(send_h, ez, split_axis=0, concat_axis=0, tiled=True)]
    ppermute x6, waiting for transfers between devices: 54.9 us -> 85.8 us  [ring_gather(): lax.ppermute(x, axis, perm=[(i, (i - d) % n) for i in range(n)])]
    all_gather x1 -> x0, waiting for transfers between devices: 19.4 us -> none  [body(): dy_z = lax.all_gather(upstream, 'z', axis=0, tiled=True)]
    all_to_all x1, starting transfers between devices: 9.71 us -> 5.15 us  [body(): lax.all_to_all(jnp.stack([upstream] * lax.axis_size('z')), 'z', 0, 0)]
    another operation x0 -> x1, local copies, waits for them, and re-layouts: none -> 4.41 us  [body(): jnp.stack([upstream] * lax.axis_size('z'))]
    unnamed x28 -> x30, local copies, waits for them, and re-layouts: 17.8 us -> 16.3 us
  transfers between devices with their start and end apart: 11 -> 10, of which waited for: 5 -> 7; matrix products, arithmetic and copies ran while one was open for 27% -> 18% of each run, Pallas kernels for 0% -> 0%
where the time goes in v1:
time: 395 us
  waiting for transfers between devices  202 us (51%)
  blocking collectives  61 us (15%)
  matrix products  49.2 us (12%)
  local copies, waits for them, and re-layouts  37.4 us (9%)
  starting transfers between devices  23.1 us (6%)
  between operations  14.3 us (4%)
  other arithmetic  7.36 us (2%)
    ppermute x6, waiting for transfers between devices, ring_gather(): lax.ppermute(x, axis, perm=[(i, (i - d) % n) for i in range(n)])  85.8 us
    all_to_all x1, waiting for transfers between devices, body(): lax.all_to_all(jnp.stack([upstream] * lax.axis_size('z')), 'z', 0, 0)  69.4 us
    all_to_all x1, blocking collectives, body(): recv_h = lax.all_to_all(send_h, ez, split_axis=0, concat_axis=0, tiled=True)  51.2 us
    reduce_scatter x1, waiting for transfers between devices, body(): lax.psum_scatter(partial, ('x', 'y'), scatter_dimension=0, tiled=True)  46 us
    dot_general x2, matrix products, part(): lax.dot_general(scaled, h_c, (((0,), (0,)), ((), ())), preferred_element_...  25.3 us
    dot_general x2, matrix products, score(): lax.dot_general(dy_c, w_full, (((1,), (0,)), ((), ())), preferred_element...  22.6 us
    unnamed x30, local copies, waits for them, and re-layouts  16.3 us
    all_to_all x1, starting transfers between devices, body(): lax.all_to_all(send_meta, ez, split_axis=0, concat_axis=0, tiled=True)  9.98 us
  transfers between devices with their start and end apart: 10, of which 7 were waited for; matrix products, arithmetic and copies ran while one was open for 18% of the time, Pallas kernels for 0%

profile of v1, /device:TPU:1, one launch (start us, length us, event | category | flops | bytes accessed | tf_op | source)
XLA Modules:
  0.0 394.8 jit_solution(5444107076643737104)
XLA Ops:
  7.2 0.8 convert_reduce_fusion.1
  10.5 10.0 %all-to-all-start.2 = ((f32[16,2,128]{2,1,0:T(2,128)}), f32[16,2,128]{2,1,0:T(2,128)S(1)}, u32[]{:S(2)}, u32[]{:S(2)}) async-start(f32[16,2,128]{2,1,0:T(2,128)} %copy.33), calls=%async_computation.2 | async-start | bytes 32768 | tf_op jit(solution)/shard_map/all_to_all | solution.py:46
  20.6 0.9 convert_reduce_fusion
  21.7 4.6 %gather_fusion = bf16[1152,768]{1,0:T(8,128)(2,1)S(1)} fusion(bf16[1024,768]{1,0:T(8,128)(2,1)S(1)} %bitcast.72, s32[2048]{0:T(1024)S(1)} %pad_clamp_fusion), kind=kCustom, calls=%fused_computation | custom fusion | bytes 3543552 | tf_op jit(solution)/shard_map/gather | solution.py:32
  26.2 1.4 broadcast_select_fusion
  27.8 51.2 %all_to_all.27 = bf16[16,72,768]{2,1,0:T(8,128)(2,1)S(1)} all-to-all(bf16[16,72,768]{2,1,0:T(8,128)(2,1)} %broadcast_select_fusion), channel_id=1, replica_groups=mesh['x'=4,'y'=4,'z'=8,'core'=2] {'z','core'}, dimensions={0} | all-to-all | bytes 3538944 | tf_op jit(solution)/shard_map/all_to_all | solution.py:45
  79.1 4.4 %stack.48 = bf16[8,128,4096]{2,1,0:T(8,128)(2,1)} broadcast(bf16[128,4096]{1,0:T(8,128)(2,1)S(1)} %copy-done.6), dimensions={1,2} | broadcast | bytes 9437184 | tf_op jit(solution)/shard_map/stack | solution.py:43
  83.5 5.2 %all-to-all-start = ((bf16[8,128,4096]{2,1,0:T(8,128)(2,1)}), bf16[8,128,4096]{2,1,0:T(8,128)(2,1)}, u32[]{:S(2)}, u32[]{:S(2)}) async-start(bf16[8,128,4096]{2,1,0:T(8,128)(2,1)} %stack.48), calls=%async_computation | async-start | bytes 16777216 | tf_op jit(solution)/shard_map/all_to_all | solution.py:43
  88.7 2.8 collective-permute-start
  92.6 16.1 %collective-permute-done = bf16[256,768]{1,0:T(8,128)(2,1)S(1)} collective-permute-done((bf16[256,768]{1,0:T(8,128)(2,1)S(1)}, bf16[256,768]{1,0:T(8,128)(2,1)S(1)}, u32[]{:S(2)}, u32[]{:S(2)}) %collective-permute-start) | collective-permute-done | bytes 393248 | tf_op jit(solution)/shard_map/ppermute | solution.py:51
  108.7 3.9 collective-permute-done.2
  112.8 1.4 bitcast_dynamic-update-slice_fusion.6
  114.2 2.5 collective-permute-start.3
  117.8 65.9 %collective-permute-done.3 = bf16[4,256,768]{2,1,0:T(8,128)(2,1)} collective-permute-done((bf16[4,256,768]{2,1,0:T(8,128)(2,1)S(1)}, bf16[4,256,768]{2,1,0:T(8,128)(2,1)}, u32[]{:S(2)}, u32[]{:S(2)}) %collective-permute-start.3) | collective-permute-done | bytes 1572896 | tf_op jit(solution)/shard_map/ppermute | solution.py:51
  183.6 2.7 bitcast_dynamic-update-slice_fusion.4
  186.3 2.6 bitcast_dynamic-update-slice_fusion.2
  188.9 2.7 bitcast_dynamic-update-slice_fusion
  191.6 1.2 bitcast_dynamic-update-slice_fusion.7
  192.9 2.7 bitcast_dynamic-update-slice_fusion.5
  195.6 2.7 bitcast_dynamic-update-slice_fusion.3
  198.3 2.6 bitcast_dynamic-update-slice_fusion.1
  200.9 6.0 %constant_dynamic-slice_fusion.2 = bf16[4,4,256,768]{3,2,1,0:T(8,128)(2,1)} fusion(bf16[8,4,256,768]{3,2,1,0:T(8,128)(2,1)} %bitcast_dynamic-update-slice_fusion.1, s32[]{:T(128)S(6)} %select_n.102), kind=kLoop, calls=%fused_computation.71 | loop fusion | bytes 12582916 | tf_op jit(solution)/shard_map/jit(_roll_dynamic)/dynamic_slice | solution.py:53
  206.9 69.4 %all-to-all-done = bf16[8,128,4096]{2,1,0:T(8,128)(2,1)} async-done(((bf16[8,128,4096]{2,1,0:T(8,128)(2,1)}), bf16[8,128,4096]{2,1,0:T(8,128)(2,1)}, u32[]{:S(2)}, u32[]{:S(2)}) %all-to-all-start) | async-done | bytes 8388640 | tf_op jit(solution)/shard_map/all_to_all | solution.py:43
  278.1 10.8 %fusion = f32[4096,768]{1,0:T(8,128)S(1)} fusion(bf16[1024,768]{1,0:T(8,128)(2,1)S(1)} %bitcast.80, bf16[1024,4096]{1,0:T(8,128)(2,1)} %bitcast, f32[1024]{0:T(1024)S(1)} %get-tuple-element.26), kind=kOutput, calls=%fused_computation.4 | convolution fusion | flops 6455033856 | bytes 22548480 | tf_op jit(solution)/shard_map/dot_general | solution.py:84
  288.8 1.0 collective-permute-done.6
  289.9 14.6 %add_convert_fusion = bf16[4096,768]{1,0:T(8,128)(2,1)} fusion(f32[4096,768]{1,0:T(8,128)S(1)} %fusion, bf16[1024,768]{1,0:T(8,128)(2,1)S(1)} %bitcast.78, bf16[1024,4096]{1,0:T(8,128)(2,1)} %collective-permute-done.6, f32[1024]{0:T(1024)S(1)} %get-tuple-element.24), kind=kOutput, calls=%fused_computation.3 | convolution fusion | flops 6461325312 | bytes 28839936 | tf_op jit(solution)/shard_map/dot_general | solution.py:84
  304.5 1.7 copy.36
  307.0 11.1 %multiply_reduce_fusion.1 = f32[1024]{0:T(1024)S(1)} fusion(bf16[1024,768]{0,1:T(8,128)(2,1)S(1)} %copy.35, bf16[1024,4096]{1,0:T(8,128)(2,1)} %bitcast, bf16[4096,768]{1,0:T(8,128)(2,1)} %bitcast.76), kind=kOutput, calls=%fused_computation.9 | convolution fusion | flops 6444809216 | bytes 16257024 | tf_op jit(solution)/shard_map/dot_general | solution.py:89
  318.1 11.5 %multiply_reduce_fusion = f32[1024]{0:T(1024)S(1)} fusion(bf16[1024,768]{0,1:T(8,128)(2,1)S(1)} %copy-done.4, bf16[1024,4096]{1,0:T(8,128)(2,1)} %collective-permute-done.6, bf16[4096,768]{1,0:T(8,128)(2,1)} %bitcast.77), kind=kOutput, calls=%fused_computation.8 | convolution fusion | flops 6444809216 | bytes 16257024 | tf_op jit(solution)/shard_map/dot_general | solution.py:89
  329.6 9.8 %all_to_all.28 = f32[16,1,128]{2,1,0:T(1,128)S(1)} all-to-all(f32[16,1,128]{2,1,0:T(1,128)S(1)} %bitcast.87), channel_id=1, replica_groups=mesh['x'=4,'y'=4,'z'=8,'core'=2] {'z','core'}, dimensions={0} | all-to-all | bytes 16384 | tf_op jit(solution)/shard_map/all_to_all | solution.py:103
  340.0 46.0 %reduce-scatter.2.cloned.1.call-done = bf16[256,768]{1,0:T(8,128)(2,1)} async-done(((bf16[4096,768]{1,0:T(8,128)(2,1)}), bf16[256,768]{1,0:T(8,128)(2,1)}) %reduce-scatter.2.cloned.1.call-update) | async-done | bytes 393232 | tf_op jit(solution)/shard_map/reduce_scatter | solution.py:95
  386.0 1.9 bitcast_convert_fusion
  (61 shorter events, 8.4 us)
Async XLA Ops:
  7.2 14.5 %copy-start = (bf16[128,8,768]{2,1,0:T(8,128)(2,1)S(1)}, bf16[128,8,768]{2,1,0:T(8,128)(2,1)}, u32[]{:S(2)}) copy-start(bf16[128,8,768]{2,1,0:T(8,128)(2,1)} %param.5) | copy-start | bytes 4718596
  10.5 17.3 %all-to-all-start.2 = ((f32[16,2,128]{2,1,0:T(2,128)}), f32[16,2,128]{2,1,0:T(2,128)S(1)}, u32[]{:S(2)}, u32[]{:S(2)}) async-start(f32[16,2,128]{2,1,0:T(2,128)} %copy.33), calls=%async_computation.2 | async-start | bytes 32768 | tf_op jit(solution)/shard_map/all_to_all | solution.py:46
  27.7 51.4 %copy-start.6 = (bf16[128,4096]{1,0:T(8,128)(2,1)S(1)}, bf16[128,4096]{1,0:T(8,128)(2,1)}, u32[]{:S(2)}) copy-start(bf16[128,4096]{1,0:T(8,128)(2,1)} %param.6) | copy-start | bytes 3145732
  83.5 5.2 %copy-start.5 = (bf16[1,256,768]{2,1,0:T(8,128)(2,1)S(1)}, bf16[1,256,768]{2,1,0:T(8,128)(2,1)}, u32[]{:S(2)}) copy-start(bf16[1,256,768]{2,1,0:T(8,128)(2,1)} %param.9) | copy-start | bytes 1179652
  83.5 192.8 %all-to-all-start = ((bf16[8,128,4096]{2,1,0:T(8,128)(2,1)}), bf16[8,128,4096]{2,1,0:T(8,128)(2,1)}, u32[]{:S(2)}, u32[]{:S(2)}) async-start(bf16[8,128,4096]{2,1,0:T(8,128)(2,1)} %stack.48), calls=%async_computation | async-start | bytes 16777216 | tf_op jit(solution)/shard_map/all_to_all | solution.py:43
  88.6 297.4 %reduce-scatter.2.cloned.1.call-start = ((), (), s32[]{:S(2)}) async-start(), calls=%async_computation.5 | async-start | bytes 6684672 | tf_op jit(solution)/shard_map/reduce_scatter | solution.py:95
  88.7 20.0 %collective-permute-start = (bf16[256,768]{1,0:T(8,128)(2,1)S(1)}, bf16[256,768]{1,0:T(8,128)(2,1)S(1)}, u32[]{:S(2)}, u32[]{:S(2)}) collective-permute-start(bf16[256,768]{1,0:T(8,128)(2,1)S(1)} %bitcast.82), channel_id=1, source_target_pairs={{0,48},{16,0},{32,16},{48,32},{1,49},{17,1},{33,17},{49,33},{2,50}... | collective-permute-start | bytes 1179656 | tf_op jit(solution)/shard_map/ppermute | solution.py:51
  91.5 17.2 %collective-permute-start.1 = (bf16[256,768]{1,0:T(8,128)(2,1)S(1)}, bf16[256,768]{1,0:T(8,128)(2,1)S(1)}, u32[]{:S(2)}, u32[]{:S(2)}) collective-permute-start(bf16[256,768]{1,0:T(8,128)(2,1)S(1)} %bitcast.83), channel_id=1, source_target_pairs={{0,32},{16,48},{32,0},{48,16},{1,33},{17,49},{33,1},{49,17},{2,34}... | collective-permute-start | bytes 1179656 | tf_op jit(solution)/shard_map/ppermute | solution.py:51
  91.9 20.8 %collective-permute-start.2 = (bf16[256,768]{1,0:T(8,128)(2,1)S(1)}, bf16[256,768]{1,0:T(8,128)(2,1)S(1)}, u32[]{:S(2)}, u32[]{:S(2)}) collective-permute-start(bf16[256,768]{1,0:T(8,128)(2,1)S(1)} %bitcast.84), channel_id=1, source_target_pairs={{0,16},{16,32},{32,48},{48,0},{1,17},{17,33},{33,49},{49,1},{2,18}... | collective-permute-start | bytes 1179656 | tf_op jit(solution)/shard_map/ppermute | solution.py:51
  114.2 69.5 %collective-permute-start.3 = (bf16[4,256,768]{2,1,0:T(8,128)(2,1)S(1)}, bf16[4,256,768]{2,1,0:T(8,128)(2,1)}, u32[]{:S(2)}, u32[]{:S(2)}) collective-permute-start(bf16[4,256,768]{2,1,0:T(8,128)(2,1)S(1)} %get-tuple-element.18), channel_id=1, source_target_pairs={{0,192},{64,0},{128,64},{192,128},{1,193},{65,1},{129,65},{193,129... | collective-permute-start | bytes 4718600 | tf_op jit(solution)/shard_map/ppermute | solution.py:51
  116.6 69.7 %collective-permute-start.4 = (bf16[4,256,768]{2,1,0:T(8,128)(2,1)S(1)}, bf16[4,256,768]{2,1,0:T(8,128)(2,1)}, u32[]{:S(2)}, u32[]{:S(2)}) collective-permute-start(bf16[4,256,768]{2,1,0:T(8,128)(2,1)S(1)} %get-tuple-element.18), channel_id=1, source_target_pairs={{0,128},{64,192},{128,0},{192,64},{1,129},{65,193},{129,1},{193,65... | collective-permute-start | bytes 4718600 | tf_op jit(solution)/shard_map/ppermute | solution.py:51
  117.2 71.8 %collective-permute-start.5 = (bf16[4,256,768]{2,1,0:T(8,128)(2,1)S(1)}, bf16[4,256,768]{2,1,0:T(8,128)(2,1)}, u32[]{:S(2)}, u32[]{:S(2)}) collective-permute-start(bf16[4,256,768]{2,1,0:T(8,128)(2,1)S(1)} %get-tuple-element.18), channel_id=1, source_target_pairs={{0,64},{64,128},{128,192},{192,0},{1,65},{65,129},{129,193},{193,1... | collective-permute-start | bytes 4718600 | tf_op jit(solution)/shard_map/ppermute | solution.py:51
  276.3 13.6 %collective-permute-start.6 = (bf16[1024,4096]{1,0:T(8,128)(2,1)}, bf16[1024,4096]{1,0:T(8,128)(2,1)}, u32[]{:S(2)}, u32[]{:S(2)}) collective-permute-start(bf16[1024,4096]{1,0:T(8,128)(2,1)} %bitcast), channel_id=1, source_target_pairs={{0,1},{1,0},{2,3},{3,2},{4,5},{5,4},{6,7},{7,6},{8,9},{9,8},{10,11... | collective-permute-start | bytes 25165832 | tf_op jit(solution)/shard_map/ppermute | solution.py:58
  278.0 10.8 %copy-start.2 = (bf16[8,128,768]{2,1,0:T(8,128)(2,1)}, bf16[8,128,768]{2,1,0:T(8,128)(2,1)S(1)}, u32[]{:S(2)}) copy-start(bf16[8,128,768]{2,1,0:T(8,128)(2,1)S(1)} %convolution_convert_fusion.1) | copy-start | bytes 4718596
  304.5 1.7 copy-start.3
  307.0 11.1 %copy-start.4 = (bf16[1024,768]{0,1:T(8,128)(2,1)S(1)}, bf16[1024,768]{0,1:T(8,128)(2,1)}, u32[]{:S(2)}) copy-start(bf16[1024,768]{0,1:T(8,128)(2,1)} %copy.36) | copy-start | bytes 4718596
  318.1 21.3 %copy-start.7 = (s32[128,8]{0,1:T(8,128)S(1)}, s32[128,8]{0,1:T(8,128)}, u32[]{:S(2)}) copy-start(s32[128,8]{0,1:T(8,128)} %param.8) | copy-start | bytes 12292
  318.1 69.8 %copy-start.1 = (bf16[128,8,768]{2,1,0:T(8,128)(2,1)S(1)}, bf16[128,8,768]{2,1,0:T(8,128)(2,1)}, u32[]{:S(2)}) copy-start(bf16[128,8,768]{2,1,0:T(8,128)(2,1)} %param.5) | copy-start | bytes 4718596
Sparse Core Ops, SparseCore 0:
  304.6 81.3 reduce-scatter.1
